TPU v7x, 256 devices: a whole 4x4x8 slice. The times are simulated.
256 devices in a mesh: grp: 8 (over z), req: 4 (over x_hi, core), tp: 8 (over y, x_lo).
Axes of the slice: x: 4 (x_hi: 2, x_lo: 2; x = x_hi * 2 + x_lo), y: 4, z: 8, core: 2. Of those that a mesh axis runs over, the one named last changes fastest.
Arguments:
- stretch_in: bfloat16 [8, 2048, 3072], P('grp', 'req', 'tp'), may hold values from -48 to 48
- norm_gain: bfloat16 [3072], replicated, may hold values from 0.099609375 to 1.8984375
- w_qkv: bfloat16 [3072, 3, 3072], P(('grp', 'req'), None, 'tp'), may hold values from -1 to 1
- w_out: bfloat16 [3072, 3072], P('tp', ('grp', 'req')), may hold values from -0.625 to 0.625
- prompt_cache: bfloat16 [8, 2, 2, 1024, 3072], P('grp', None, None, 'req', 'tp'), may hold values from -6 to 6
- prompt_len: int32 [8], replicated, may hold values from 256 to 1024, as said below
- req_count: int32 [8], replicated, may hold values from 8 to 16, as said below
- req_map: int32 [8, 16], replicated, may hold values from -1 to 31, as said below
- prefix_len: int32 [8, 16], replicated, may hold values from 1 to 1024, as said below
- slot_query: bfloat16 [32, 8, 2, 3072], P(('grp', 'req'), None, None, 'tp'), may hold values from -8 to 8
- slot_new_kv: bfloat16 [32, 8, 2, 2, 3072], P(('grp', 'req'), None, None, None, 'tp'), may hold values from -6 to 6
Outputs:
- stretch_branch: bfloat16 [8, 2048, 3072], P('grp', 'req', 'tp')
- slot_out: bfloat16 [32, 8, 2, 3072], P(('grp', 'req'), None, None, 'tp')
Inputs may be any that keep to these rules, and one draw needn't show every extreme that they name: `prompt_len`: some group's prompt fills all 1024 positions. prefix_len[g, r] <= prompt_len[g]; request 0 of every group attends to its whole prompt. `req_count`: some group has 16 requests. `req_map`: entries of requests that are not live are -1; every replica serves at most 8 live requests, and some replica exactly 8.
All inputs are finite; a program needn't handle non-finite values.
Results may differ from a plain program's by a relative error of at most 0.02.
Values may be sent and summed in bfloat16 or wider, within the bound.
No kernel may reach another device: no remote copies, remote signals or barrier semaphores. Data moves between devices by JAX's collectives and lax.ppermute only.
A program may use at most 128 MiB of HBM per device.

v0:
```python
import jax
import jax.numpy as jnp
from jax import lax
from jax.sharding import PartitionSpec as P

HD = 96


NEG_FLOOR = -1e30
NORM_EPS = 1e-05
ROPE_BASE = 10000.0


def merged_2(value, axis, combine):
    everything = jax.tree.map(lambda part: lax.all_gather(part, axis), value)
    first = jax.tree.map(lambda part: part[0], everything)

    def turn(k, so_far):
        return combine(so_far, jax.tree.map(lambda part: part[k], everything))

    return lax.fori_loop(1, lax.axis_size(axis), turn, first)


def rope_angles(positions, head_size):
    half_size = head_size // 2
    freqs = ROPE_BASE ** (-(jnp.arange(half_size, dtype=jnp.float32) * 2.0 / head_size))
    angles = positions.astype(jnp.float32)[:, None] * freqs[None, :]
    return (jnp.cos(angles), jnp.sin(angles))


def rotate_pairs(values, cosine, sine_table):
    half_size = values.shape[-1] // 2
    first_half = values[..., :half_size]
    second_half = values[..., half_size:]
    cos_b = cosine[:, None, :]
    sin_b = sine_table[:, None, :]
    return jnp.concatenate(
        [first_half * cos_b - second_half * sin_b, second_half * cos_b + first_half * sin_b],
        axis=-1,
    )


def exact_round(values):
    return lax.optimization_barrier(values.astype(jnp.bfloat16)).astype(jnp.float32)


def merge_soft(first_state, second_state):
    peak_one, total_one, accum_one = first_state
    peak_two, total_two, accum_two = second_state
    peak_new = jnp.maximum(peak_one, peak_two)
    factor_one = jnp.exp(peak_one - peak_new)
    factor_two = jnp.exp(peak_two - peak_new)
    return (
        peak_new,
        total_one * factor_one + total_two * factor_two,
        accum_one * factor_one[..., None] + accum_two * factor_two[..., None],
    )


def cache_partial(queries, cache_keys, cache_values, allowed, scale_factor):
    scores = (
        jnp.einsum("slhe,lkhe->slhk", queries, cache_keys, preferred_element_type=jnp.float32)
        * scale_factor
    )
    key_gate = allowed[:, None, None, :]
    masked = jnp.where(key_gate, scores, NEG_FLOOR)
    row_peak = jnp.max(masked, axis=3)
    weights = jnp.where(key_gate, jnp.exp(masked - row_peak[..., None]), 0.0)
    totals = jnp.sum(weights, axis=3)
    accumulated = jnp.einsum(
        "slhk,lkhe->slhe",
        weights.astype(jnp.bfloat16),
        cache_values,
        preferred_element_type=jnp.float32,
    )
    return (row_peak, totals, accumulated)


def finish_slots(merged, own_query, own_kv, own_alive, scale_factor):
    row_peak, totals, accumulated = merged
    own_key = own_kv[:, :, 0]
    own_value = own_kv[:, :, 1]
    own_score = (
        jnp.einsum("slhe,slhe->slh", own_query, own_key, preferred_element_type=jnp.float32)
        * scale_factor
    )
    new_peak = jnp.maximum(row_peak, own_score)
    shrink = jnp.exp(row_peak - new_peak)
    own_weight = jnp.exp(own_score - new_peak)
    new_total = totals * shrink + own_weight
    mixed = accumulated * shrink[..., None] + exact_round(own_weight)[..., None] * own_value.astype(
        jnp.float32
    )
    result = mixed / new_total[..., None]
    result = jnp.where(own_alive[:, None, None, None], result, 0.0)
    return result.astype(jnp.bfloat16)


def per_device(
    stretch_in,
    norm_gain,
    w_qkv,
    w_out,
    prompt_cache,
    prompt_len,
    req_count,
    req_map,
    prefix_len,
    slot_query,
    slot_new_kv,
):
    group_id = lax.axis_index("grp")
    block_id = lax.axis_index("req")
    replica_id = lax.axis_index(("grp", "req"))
    replicas = lax.axis_size(("grp", "req"))
    stretch_rows = stretch_in.shape[1]
    tensor_width = stretch_in.shape[2]
    head_size = HD
    local_heads = tensor_width // head_size
    cache_rows = prompt_cache.shape[3]
    layer_count = prompt_cache.shape[1]
    scale_factor = head_size ** (-0.5)
    length = lax.dynamic_index_in_dim(prompt_len, group_id, 0, keepdims=False)
    full_rows = lax.all_gather(stretch_in[0], "tp", axis=1, tiled=True)
    widened = full_rows.astype(jnp.float32)
    mean_square = jnp.mean(widened * widened, axis=1, keepdims=True)
    normed = (widened * lax.rsqrt(mean_square + NORM_EPS) * norm_gain.astype(jnp.float32)).astype(
        jnp.bfloat16
    )
    weight_piece = lax.all_gather(w_qkv, ("grp", "req"), axis=0, tiled=True)
    projected = jnp.dot(
        normed, weight_piece.reshape(weight_piece.shape[0], -1), preferred_element_type=jnp.float32
    )
    projected = projected.reshape(stretch_rows, 3, local_heads, head_size)
    query_pos = block_id * stretch_rows + jnp.arange(stretch_rows, dtype=jnp.int32)
    cosine, sine_table = rope_angles(length + query_pos, head_size)
    queries = rotate_pairs(projected[:, 0], cosine, sine_table).astype(jnp.bfloat16)
    new_keys = rotate_pairs(projected[:, 1], cosine, sine_table).astype(jnp.bfloat16)
    new_values = projected[:, 2].astype(jnp.bfloat16)
    fresh_kv = jnp.stack(
        [
            new_keys.reshape(stretch_rows, tensor_width),
            new_values.reshape(stretch_rows, tensor_width),
        ],
        axis=0,
    )
    local_kv = jnp.concatenate([prompt_cache[0, 0], fresh_kv], axis=1)
    block_span = cache_rows + stretch_rows

    def attend_rows(carry, kv_piece, first_row):
        row_peak, totals, accumulated = carry
        piece_rows = kv_piece.shape[1]
        row_index = first_row + jnp.arange(piece_rows, dtype=jnp.int32)
        shard_index = row_index // block_span
        offset = row_index % block_span
        from_cache = offset < cache_rows
        cache_pos = shard_index * cache_rows + offset
        stretch_pos = shard_index * stretch_rows + offset - cache_rows
        allowed = jnp.where(
            from_cache[None, :],
            cache_pos[None, :] < length,
            stretch_pos[None, :] <= query_pos[:, None],
        )
        piece_keys = kv_piece[0].reshape(piece_rows, local_heads, head_size)
        piece_values = kv_piece[1].reshape(piece_rows, local_heads, head_size)
        scores = (
            jnp.einsum("qhe,khe->hqk", queries, piece_keys, preferred_element_type=jnp.float32)
            * scale_factor
        )
        key_gate = allowed[None]
        masked = jnp.where(key_gate, scores, NEG_FLOOR)
        new_peak = jnp.maximum(row_peak, jnp.max(masked, axis=2))
        shrink = jnp.exp(row_peak - new_peak)
        weights = jnp.where(key_gate, jnp.exp(masked - new_peak[..., None]), 0.0)
        totals = totals * shrink + jnp.sum(weights, axis=2)
        update = jnp.einsum(
            "hqk,khe->qhe",
            weights.astype(jnp.bfloat16),
            piece_values,
            preferred_element_type=jnp.float32,
        )
        accumulated = accumulated * jnp.transpose(shrink)[:, :, None] + update
        return (new_peak, totals, accumulated)

    start_state = (
        jnp.full((local_heads, stretch_rows), NEG_FLOOR, jnp.float32),
        jnp.zeros((local_heads, stretch_rows), jnp.float32),
        jnp.zeros((stretch_rows, local_heads, head_size), jnp.float32),
    )
    kv_piece = lax.all_gather(local_kv, "req", axis=1, tiled=True)
    piece_rows = kv_piece.shape[1]

    def one_block(block_step, inner_state):
        part_kv = lax.dynamic_slice_in_dim(kv_piece, block_step * block_span, block_span, 1)
        return attend_rows(inner_state, part_kv, block_step * block_span)

    row_peak, totals, accumulated = lax.fori_loop(
        0, piece_rows // block_span, one_block, start_state
    )
    attended = (
        (accumulated / jnp.transpose(totals)[:, :, None])
        .astype(jnp.bfloat16)
        .reshape(stretch_rows, tensor_width)
    )
    partial_sum = jnp.dot(
        attended,
        lax.all_gather(w_out, ("grp", "req"), axis=1, tiled=True),
        preferred_element_type=jnp.float32,
    ).astype(jnp.bfloat16)
    branch = lax.psum_scatter(
        partial_sum.astype(jnp.float32).astype(jnp.bfloat16), "tp", scatter_dimension=1, tiled=True
    )
    group_total = req_count.shape[0]
    max_requests = req_map.shape[1]
    flat_count = group_total * max_requests
    slot_count = slot_query.shape[1]
    request_ids = jnp.arange(flat_count, dtype=jnp.int32)
    group_of = request_ids // max_requests
    count_of = jnp.sum(
        jnp.where(
            group_of[:, None] == jnp.arange(group_total, dtype=jnp.int32)[None, :],
            req_count[None, :],
            0,
        ),
        axis=1,
    )
    request_live = request_ids % max_requests < count_of
    flat_map = req_map.reshape(flat_count)
    member = (flat_map[None, :] == jnp.arange(replicas, dtype=jnp.int32)[:, None]) & request_live[
        None, :
    ]
    order_rank = jnp.cumsum(member.astype(jnp.int32), axis=1) - 1
    slot_hit = member[:, None, :] & (
        order_rank[:, None, :] == jnp.arange(slot_count, dtype=jnp.int32)[None, :, None]
    )
    slot_request = jnp.sum(jnp.where(slot_hit, request_ids[None, None, :], 0), axis=2).reshape(
        replicas * slot_count
    )
    slot_alive = jnp.any(slot_hit, axis=2).reshape(replicas * slot_count)
    prefix_flat = prefix_len.reshape(flat_count)
    own_query = slot_query[0].reshape(slot_count, layer_count, local_heads, head_size)
    own_kv = slot_new_kv[0].reshape(slot_count, layer_count, 2, local_heads, head_size)
    own_alive = lax.dynamic_slice_in_dim(slot_alive, replica_id * slot_count, slot_count, 0)
    cache_keys = prompt_cache[0, :, 0].reshape(layer_count, cache_rows, local_heads, head_size)
    cache_values = prompt_cache[0, :, 1].reshape(layer_count, cache_rows, local_heads, head_size)
    cache_pos = block_id * cache_rows + jnp.arange(cache_rows, dtype=jnp.int32)
    all_queries = lax.all_gather(slot_query[0], ("grp", "req"), axis=0, tiled=True)
    all_queries = all_queries.reshape(replicas * slot_count, layer_count, local_heads, head_size)
    slot_group = slot_request // max_requests
    slot_prefix = jnp.sum(jnp.where(slot_hit, prefix_flat[None, None, :], 0), axis=2).reshape(
        replicas * slot_count
    )
    allowed = (
        slot_alive[:, None]
        & (slot_group[:, None] == group_id)
        & (cache_pos[None, :] < slot_prefix[:, None])
    )
    local_part = cache_partial(all_queries, cache_keys, cache_values, allowed, scale_factor)
    every_slot = merged_2(local_part, ("grp", "req"), merge_soft)
    merged = tuple(
        (
            lax.dynamic_slice_in_dim(member_state, replica_id * slot_count, slot_count, 0)
            for member_state in every_slot
        )
    )
    result = finish_slots(merged, own_query, own_kv, own_alive, scale_factor)
    return (branch[None], result.reshape(slot_count, layer_count, tensor_width)[None])


def solution(mesh):
    placed = (
        P("grp", "req", "tp"),
        P(),
        P(("grp", "req"), None, "tp"),
        P("tp", ("grp", "req")),
        P("grp", None, None, "req", "tp"),
        P(),
        P(),
        P(),
        P(),
        P(("grp", "req"), None, None, "tp"),
        P(("grp", "req"), None, None, None, "tp"),
    )
    return jax.shard_map(
        per_device,
        mesh=mesh,
        in_specs=placed,
        out_specs=(P("grp", "req", "tp"), P(("grp", "req"), None, None, "tp")),
        check_vma=False,
    )
```

profile of v0, /device:TPU:1, one launch (start us, length us, event | category | flops | bytes accessed | tf_op | source)
XLA Modules:
  0.0 780.4 jit_solution(8010306654811472734)
XLA Ops:
  13.7 73.5 %all-gather.17.cloned.1.call-done = bf16[1,512,3072]{2,1,0:T(8,128)(2,1)} async-done(((bf16[1,512,384]{2,1,0:T(8,128)(2,1)}), bf16[1,512,3072]{2,1,0:T(8,128)(2,1)}) %all-gather.17.cloned.1.call-update) | async-done | bytes 3145744 | tf_op jit(solution)/shard_map/all_gather | solution.py:124
  87.2 2.6 fusion.29
  89.8 97.2 %all-gather.11.cloned.1.call-done = bf16[3072,3,384]{2,0,1:T(8,128)(2,1)} async-done(((bf16[96,3,384]{2,0,1:T(8,128)(2,1)}), bf16[3072,3,384]{2,0,1:T(8,128)(2,1)}) %all-gather.11.cloned.1.call-update) | async-done | bytes 7077904 | tf_op jit(solution)/shard_map/all_gather | solution.py:130
  187.0 10.1 %copy.66 = bf16[3072,3,384]{0,2,1:T(8,128)(2,1)} copy(bf16[3072,3,384]{2,0,1:T(8,128)(2,1)} %all-gather.11.cloned.1.call-done) | data formatting | bytes 14155776 | tf_op jit(solution)/shard_map/all_gather | solution.py:130
  197.1 6.2 fusion.33
  206.4 40.3 %all-gather.13.cloned.1.call-done = bf16[2,3072,384]{1,2,0:T(8,128)(2,1)} async-done(((bf16[2,768,384]{1,2,0:T(8,128)(2,1)}), bf16[2,3072,384]{1,2,0:T(8,128)(2,1)}) %all-gather.13.cloned.1.call-update) | async-done | bytes 4718608 | tf_op jit(solution)/shard_map/all_gather | solution.py:190
  246.7 53.7 %while.40 = (s32[]{:T(128)}, f32[4,512]{1,0:T(4,128)S(1)}, f32[4,512]{1,0:T(4,128)S(1)}, f32[512,4,96]{0,2,1:T(8,128)S(1)}, s32[]{:T(128)}, /*index=5*/bf16[2,30...) while((s32[]{:T(128)}, f32[4,512]{1,0:T(4,128)S(1)}, ...), condition=%wide.region_4.5_spmd.clone, body=%wide.region_1.4_spmd.clone.sunk | while | flops 625841408 | bytes 51262716 | solution.py:197
  248.2 1.3 constant_dynamic-slice_fusion.7
  249.5 4.0 fusion.90
  253.5 4.5 fusion.92
  258.1 1.9 fusion.94
  261.5 1.3 constant_dynamic-slice_fusion.7
  262.9 4.0 fusion.90
  266.9 4.5 fusion.92
  271.5 1.9 fusion.94
  274.9 1.3 constant_dynamic-slice_fusion.7
  276.3 4.0 fusion.90
  280.3 4.5 fusion.92
  284.9 1.9 fusion.94
  289.6 4.0 fusion.90
  293.7 4.5 fusion.92
  298.5 1.9 fusion.94
  300.5 28.8 %all-gather.15.cloned.1.call-done = bf16[384,3072]{0,1:T(8,128)(2,1)} async-done(((bf16[384,96]{0,1:T(8,128)(2,1)}), bf16[384,3072]{0,1:T(8,128)(2,1)}) %all-gather.15.cloned.1.call-update) | async-done | bytes 2359312 | tf_op jit(solution)/shard_map/all_gather | solution.py:207
  329.3 3.5 convolution_convert_fusion
  332.8 2.8 copy.90
  339.3 40.1 %all-gather.1 = bf16[1,256,2,384]{3,2,0,1:T(2,128)(2,1)S(1)} all-gather(bf16[1,8,2,384]{3,2,0,1:T(2,128)(2,1)S(1)} %bitcast.152), channel_id=3, replica_groups=mesh['grp'=8,'req'=4,'tp'=8] {'grp','req'}, dimensions={1}, use_global_device_ids=true | all-gather | bytes 405504 | tf_op jit(solution)/shard_map/all_gather | solution.py:247
  380.7 1.5 convolution_bitcast_fusion
  382.3 39.7 %all-gather.2 = f32[8192,2,4]{0,2,1:T(4,128)S(1)} all-gather(f32[256,2,4]{0,2,1:T(4,128)S(1)} %get-tuple-element.509), channel_id=4, replica_groups=mesh['grp'=8,'req'=4,'tp'=8] {'grp','req'}, dimensions={0}, use_global_device_ids=true | all-gather | bytes 270336 | tf_op jit(solution)/shard_map/all_gather | solution.py:15
  422.7 39.1 %all-gather.3 = f32[8192,2,4]{0,2,1:T(4,128)S(1)} all-gather(f32[256,2,4]{0,2,1:T(4,128)S(1)} %fusion.40), channel_id=5, replica_groups=mesh['grp'=8,'req'=4,'tp'=8] {'grp','req'}, dimensions={0}, use_global_device_ids=true | all-gather | bytes 270336 | tf_op jit(solution)/shard_map/all_gather | solution.py:15
  462.6 1.9 copy.91
  464.5 150.5 %all-gather.19.cloned.1.call-done = f32[8192,2,4,96]{0,3,2,1:T(8,128)} async-done(((f32[256,2,4,96]{0,3,2,1:T(8,128)}), f32[8192,2,4,96]{0,3,2,1:T(8,128)}) %all-gather.19.cloned.1.call-update) | async-done | bytes 25165840 | tf_op jit(solution)/shard_map/all_gather | solution.py:15
  616.8 34.1 %copy.88 = f32[8192,2,4,96]{3,2,1,0:T(4,128)} copy(f32[8192,2,4,96]{0,3,2,1:T(8,128)} %all-gather.19.cloned.1.call-done) | data formatting | bytes 50331648 | tf_op jit(solution)/shard_map/while | solution.py:21
  650.9 121.5 %while.39 = (s32[]{:T(128)}, f32[256,2,4]{0,2,1:T(4,128)S(1)}, f32[256,2,4]{0,2,1:T(4,128)S(1)}, f32[256,2,4,96]{3,2,1,0:T(4,128)S(1)}, f32[32,256,2,4]{1,0,3,2:...) while((s32[]{:T(128)}, f32[256,2,4]{0,2,1:T(4,128)S(1)}, ...), condition=%wide.region_14.15_spmd, body=%wide.region_13.14_spmd.sunk | while | flops 602117 | bytes 2506903 | solution.py:21
  651.3 3.5 fusion.85
  655.2 3.5 fusion.85
  659.2 3.5 fusion.85
  663.1 3.5 fusion.85
  667.0 3.5 fusion.85
  670.9 3.5 fusion.85
  674.8 3.5 fusion.85
  678.7 3.5 fusion.85
  682.7 3.5 fusion.85
  686.6 3.5 fusion.85
  690.5 3.5 fusion.85
  694.4 3.5 fusion.85
  698.3 3.5 fusion.85
  702.3 3.5 fusion.85
  706.2 3.5 fusion.85
  710.1 3.5 fusion.85
  714.0 3.5 fusion.85
  717.9 3.5 fusion.85
  721.9 3.5 fusion.85
  725.8 3.5 fusion.85
  729.7 3.5 fusion.85
  733.6 3.5 fusion.85
  737.5 3.5 fusion.85
  741.5 3.5 fusion.85
  745.4 3.5 fusion.85
  749.3 3.5 fusion.85
  753.2 3.5 fusion.85
  757.1 3.5 fusion.85
  761.1 3.5 fusion.85
  765.0 3.5 fusion.85
  768.9 3.5 fusion.85
  (250 shorter events, 39.2 us)
Async XLA Ops:
  7.2 80.0 %all-gather.17.cloned.1.call-start = ((), (), s32[]{:S(2)}) async-start(), calls=%async_computation.4 | async-start | bytes 3538944 | tf_op jit(solution)/shard_map/all_gather | solution.py:124
  7.9 179.1 %all-gather.11.cloned.1.call-start = ((), (), s32[]{:S(2)}) async-start(), calls=%async_computation.1 | async-start | bytes 7299072 | tf_op jit(solution)/shard_map/all_gather | solution.py:130
  8.6 238.0 %all-gather.13.cloned.1.call-start = ((), (), s32[]{:S(2)}) async-start(), calls=%async_computation.2 | async-start | bytes 5898240 | tf_op jit(solution)/shard_map/all_gather | solution.py:190
  89.8 107.3 %copy-start.1 = (bf16[1,512,3072]{2,1,0:T(8,128)(2,1)S(1)}, bf16[1,512,3072]{2,1,0:T(8,128)(2,1)}, u32[]{:S(2)}) copy-start(bf16[1,512,3072]{2,1,0:T(8,128)(2,1)} %all-gather.17.cloned.1.call-done) | copy-start | bytes 9437188
  203.3 0.9 copy-start.3
  203.4 0.9 copy-start.4
  205.7 123.6 %all-gather.15.cloned.1.call-start = ((), (), s32[]{:S(2)}) async-start(), calls=%async_computation.3 | async-start | bytes 2433024 | tf_op jit(solution)/shard_map/all_gather | solution.py:207
  206.3 256.3 %reduce-scatter.4.cloned.1.call-start = ((), (), s32[]{:S(2)}) async-start(), calls=%async_computation.6 | async-start | bytes 3538944
  253.5 4.6 copy-start
  266.9 4.6 copy-start
  280.3 4.6 copy-start
  293.7 4.8 copy-start
  335.6 0.7 copy-start.7
  335.6 0.8 copy-start.9
  335.6 1.2 copy-start.8
  335.6 3.3 copy-start.2
  335.6 3.6 copy-start.5
  335.7 279.4 %all-gather.19.cloned.1.call-start = ((), (), s32[]{:S(2)}) async-start(), calls=%async_computation.5 | async-start | bytes 25952256 | tf_op jit(solution)/shard_map/all_gather | solution.py:15
  382.3 79.9 %copy-start.6 = (bf16[1,8,2,2,384]{4,3,2,1,0:T(2,128)(2,1)S(1)}, bf16[1,8,2,2,384]{4,3,2,1,0:T(2,128)(2,1)}, u32[]{:S(2)}) copy-start(bf16[1,8,2,2,384]{4,3,2,1,0:T(2,128)(2,1)} %param.25) | copy-start | bytes 73732
Sparse Core Ops, SparseCore 0:
  9.8 77.3 all-gather.16
  90.0 96.9 all-gather.10
  205.8 40.7 all-gather.12
  249.3 79.9 all-gather.14
  335.8 76.0 reduce-scatter.3
  414.3 200.6 all-gather.18
where the time goes:
time: 784 us; the launch traced here: 780 us
  waiting for transfers between devices  392 us (50%)
  other arithmetic  142 us (18%)
  blocking collectives  119 us (15%)
  local copies, waits for them, and re-layouts  75.2 us (10%)
  matrix products  35.5 us (5%)
  between operations  14.4 us (2%)
    all_gather x1, waiting for transfers between devices, merged_2(): everything = jax.tree.map(lambda part: lax.all_gather(part, axis), value)  151 us
    add x31, other arithmetic, merge_soft(): accum_one * factor_one[..., None] + accum_two * factor_two[..., None]  107 us
    all_gather x1, waiting for transfers between devices, per_device(): weight_piece = lax.all_gather(w_qkv, ('grp', 'req'), axis=0, tiled=True)  97.2 us
    all_gather x2, blocking collectives, merged_2(): everything = jax.tree.map(lambda part: lax.all_gather(part, axis), value)  78.9 us
    all_gather x1, waiting for transfers between devices, per_device(): full_rows = lax.all_gather(stretch_in[0], 'tp', axis=1, tiled=True)  73.5 us
    all_gather x1, waiting for transfers between devices, per_device(): kv_piece = lax.all_gather(local_kv, 'req', axis=1, tiled=True)  40.3 us
    all_gather x1, blocking collectives, per_device(): lax.all_gather(slot_query[0], ('grp', 'req'), axis=0, tiled=True)  40.1 us
    while x2, local copies, waits for them, and re-layouts, merged_2(): return lax.fori_loop(1, lax.axis_size(axis), turn, first)  34.6 us
  transfers between devices with their start and end apart: 6, of which 5 were waited for; matrix products, arithmetic and copies ran while one was open for 9% of the time, Pallas kernels for 0%

commit v1 on v0

--- a/solution.py
+++ b/solution.py
@@ -202,16 +202,17 @@
         .astype(jnp.bfloat16)
         .reshape(stretch_rows, tensor_width)
     )
-    partial_sum = jnp.dot(
+    out_weight_t = lax.all_gather(jnp.transpose(w_out), ("grp", "req"), axis=0, tiled=True)
+    partial_sum = lax.dot_general(
         attended,
-        lax.all_gather(w_out, ("grp", "req"), axis=1, tiled=True),
+        out_weight_t,
+        (((1,), (1,)), ((), ())),
         preferred_element_type=jnp.float32,
     ).astype(jnp.bfloat16)
     branch = lax.psum_scatter(
         partial_sum.astype(jnp.float32).astype(jnp.bfloat16), "tp", scatter_dimension=1, tiled=True
     )
-    group_total = req_count.shape[0]
-    max_requests = req_map.shape[1]
+    group_total, max_requests = req_map.shape
     flat_count = group_total * max_requests
     slot_count = slot_query.shape[1]
     request_ids = jnp.arange(flat_count, dtype=jnp.int32)
@@ -226,43 +227,53 @@
     )
     request_live = request_ids % max_requests < count_of
     flat_map = req_map.reshape(flat_count)
-    member = (flat_map[None, :] == jnp.arange(replicas, dtype=jnp.int32)[:, None]) & request_live[
-        None, :
-    ]
-    order_rank = jnp.cumsum(member.astype(jnp.int32), axis=1) - 1
-    slot_hit = member[:, None, :] & (
-        order_rank[:, None, :] == jnp.arange(slot_count, dtype=jnp.int32)[None, :, None]
-    )
-    slot_request = jnp.sum(jnp.where(slot_hit, request_ids[None, None, :], 0), axis=2).reshape(
-        replicas * slot_count
-    )
-    slot_alive = jnp.any(slot_hit, axis=2).reshape(replicas * slot_count)
+    earlier = (
+        (flat_map[None, :] == flat_map[:, None])
+        & request_live[None, :]
+        & (request_ids[None, :] < request_ids[:, None])
+    )
+    order_rank = jnp.sum(earlier.astype(jnp.int32), axis=1)
+    slot_of = jnp.where(request_live, flat_map * slot_count + order_rank, 0)
     prefix_flat = prefix_len.reshape(flat_count)
-    own_query = slot_query[0].reshape(slot_count, layer_count, local_heads, head_size)
-    own_kv = slot_new_kv[0].reshape(slot_count, layer_count, 2, local_heads, head_size)
-    own_alive = lax.dynamic_slice_in_dim(slot_alive, replica_id * slot_count, slot_count, 0)
+    first_request = group_id * max_requests
+    mine_live = lax.dynamic_slice_in_dim(request_live, first_request, max_requests, 0)
+    mine_slot = lax.dynamic_slice_in_dim(slot_of, first_request, max_requests, 0)
+    mine_prefix = lax.dynamic_slice_in_dim(prefix_flat, first_request, max_requests, 0)
+    all_queries = lax.all_gather(
+        slot_query[0].reshape(slot_count, layer_count * tensor_width), ("grp", "req"), axis=0, tiled=True
+    )
+    picked = jnp.take(all_queries, mine_slot, axis=0).reshape(
+        max_requests, layer_count, local_heads, head_size
+    )
     cache_keys = prompt_cache[0, :, 0].reshape(layer_count, cache_rows, local_heads, head_size)
     cache_values = prompt_cache[0, :, 1].reshape(layer_count, cache_rows, local_heads, head_size)
     cache_pos = block_id * cache_rows + jnp.arange(cache_rows, dtype=jnp.int32)
-    all_queries = lax.all_gather(slot_query[0], ("grp", "req"), axis=0, tiled=True)
-    all_queries = all_queries.reshape(replicas * slot_count, layer_count, local_heads, head_size)
-    slot_group = slot_request // max_requests
-    slot_prefix = jnp.sum(jnp.where(slot_hit, prefix_flat[None, None, :], 0), axis=2).reshape(
-        replicas * slot_count
-    )
-    allowed = (
-        slot_alive[:, None]
-        & (slot_group[:, None] == group_id)
-        & (cache_pos[None, :] < slot_prefix[:, None])
-    )
-    local_part = cache_partial(all_queries, cache_keys, cache_values, allowed, scale_factor)
-    every_slot = merged_2(local_part, ("grp", "req"), merge_soft)
-    merged = tuple(
-        (
-            lax.dynamic_slice_in_dim(member_state, replica_id * slot_count, slot_count, 0)
-            for member_state in every_slot
-        )
-    )
+    allowed = mine_live[:, None] & (cache_pos[None, :] < mine_prefix[:, None])
+    part_peak, part_total, part_accum = cache_partial(
+        picked, cache_keys, cache_values, allowed, scale_factor
+    )
+    packed = jnp.concatenate([part_peak[..., None], part_total[..., None], part_accum], axis=-1)
+    block_parts = lax.all_gather(packed, "req", axis=0)
+    peaks = block_parts[..., 0]
+    group_peak = jnp.max(peaks, axis=0)
+    factor = jnp.exp(peaks - group_peak[None])
+    group_total_w = jnp.sum(block_parts[..., 1] * factor, axis=0)
+    group_accum = jnp.sum(block_parts[..., 2:] * factor[..., None], axis=0)
+    merged_group = jnp.concatenate(
+        [group_peak[..., None], group_total_w[..., None], group_accum], axis=-1
+    )
+    every_group = lax.all_gather(merged_group, "grp", axis=0, tiled=True)
+    slot_hit = (
+        request_live[None, :]
+        & (flat_map[None, :] == replica_id)
+        & (order_rank[None, :] == jnp.arange(slot_count, dtype=jnp.int32)[:, None])
+    )
+    own_request = jnp.sum(jnp.where(slot_hit, request_ids[None, :], 0), axis=1)
+    own_alive = jnp.any(slot_hit, axis=1)
+    own_state = jnp.take(every_group, own_request, axis=0)
+    merged = (own_state[..., 0], own_state[..., 1], own_state[..., 2:])
+    own_query = slot_query[0].reshape(slot_count, layer_count, local_heads, head_size)
+    own_kv = slot_new_kv[0].reshape(slot_count, layer_count, 2, local_heads, head_size)
     result = finish_slots(merged, own_query, own_kv, own_alive, scale_factor)
     return (branch[None], result.reshape(slot_count, layer_count, tensor_width)[None])
 

time: 784 us -> 426 us (0.54)
  waiting for transfers between devices: 392 us -> 243 us
  other arithmetic: 142 us -> 31.8 us
  blocking collectives: 119 us -> 70.4 us
  local copies, waits for them, and re-layouts: 75.2 us -> 28.9 us
    all_gather x2 -> x1, waiting for transfers between devices: 179 us -> 29.6 us  [per_device(): lax.all_gather(jnp.transpose(w_out), ('grp', 'req'), axis=0, tiled=True)]
    add x63 -> x0, other arithmetic: 108 us -> none  [the longest x31 107 us: merge_soft(): accum_one * factor_one[..., None] + accum_two * factor_two[..., None]]
    all_gather x3, blocking collectives: 119 us -> 70.4 us  [the longest x1 40.3 us: per_device(): lax.all_gather(slot_query[0].reshape(slot_count, layer_count * tensor_wid...]
    while x14 -> x12, local copies, waits for them, and re-layouts: 35.2 us -> 0.3 us  [the longest x2 34.6 us: merged_2(): return lax.fori_loop(1, lax.axis_size(axis), turn, first)]
    exp x62 -> x0, local copies, waits for them, and re-layouts: 11.1 us -> none  [the longest x31 5.61 us: merge_soft(): factor_one = jnp.exp(peak_one - peak_new)]
  transfers between devices with their start and end apart: 6 -> 5, of which waited for: 5 -> 4; matrix products, arithmetic and copies ran while one was open for 9% -> 16% of each run, Pallas kernels for 0% -> 0%
where the time goes in v1:
time: 426 us; the launch traced here: 422 us
  waiting for transfers between devices  243 us (57%)
  blocking collectives  70.4 us (17%)
  matrix products  33.9 us (8%)
  other arithmetic  31.8 us (7%)
  local copies, waits for them, and re-layouts  28.9 us (7%)
  between operations  14.2 us (3%)
    all_gather x1, waiting for transfers between devices, per_device(): weight_piece = lax.all_gather(w_qkv, ('grp', 'req'), axis=0, tiled=True)  97.2 us
    all_gather x1, waiting for transfers between devices, per_device(): full_rows = lax.all_gather(stretch_in[0], 'tp', axis=1, tiled=True)  73.7 us
    all_gather x1, blocking collectives, per_device(): lax.all_gather(slot_query[0].reshape(slot_count, layer_count * tensor_wid...  40.3 us
    all_gather x1, waiting for transfers between devices, per_device(): kv_piece = lax.all_gather(local_kv, 'req', axis=1, tiled=True)  40.3 us
    all_gather x1, waiting for transfers between devices, per_device(): lax.all_gather(jnp.transpose(w_out), ('grp', 'req'), axis=0, tiled=True)  29.6 us
    all_gather x1, blocking collectives, per_device(): every_group = lax.all_gather(merged_group, 'grp', axis=0, tiled=True)  20.9 us
    reduce_sum x4, other arithmetic, attend_rows(): totals = totals * shrink + jnp.sum(weights, axis=2)  17.9 us
    dot_general x4, matrix products, attend_rows(): jnp.einsum('qhe,khe->hqk', queries, piece_keys, preferred_element_type=jn...  16 us
  transfers between devices with their start and end apart: 5, of which 4 were waited for; matrix products, arithmetic and copies ran while one was open for 16% of the time, Pallas kernels for 0%

profile of v1, /device:TPU:1, one launch (start us, length us, event | category | flops | bytes accessed | tf_op | source)
XLA Modules:
  0.0 422.4 jit_solution(4929669791209313145)
XLA Ops:
  7.2 0.7 all-gather.13.cloned.1.call-update
  7.9 0.7 all-gather.7.cloned.1.call-update
  8.7 0.7 convert_element_type.79
  9.4 1.0 slice.75
  10.4 0.2 copy.94
  10.6 1.2 dynamic_slice.23
  11.9 0.6 add_convert_fusion.2
  12.4 1.1 multiply_cosine_fusion
  13.5 73.7 %all-gather.13.cloned.1.call-done = bf16[1,512,3072]{2,1,0:T(8,128)(2,1)} async-done(((bf16[1,512,384]{2,1,0:T(8,128)(2,1)}), bf16[1,512,3072]{2,1,0:T(8,128)(2,1)}) %all-gather.13.cloned.1.call-update) | async-done | bytes 3145744 | tf_op jit(solution)/shard_map/all_gather | solution.py:124
  87.2 2.6 fusion.25
  89.8 97.2 %all-gather.7.cloned.1.call-done = bf16[3072,3,384]{2,0,1:T(8,128)(2,1)} async-done(((bf16[96,3,384]{2,0,1:T(8,128)(2,1)}), bf16[3072,3,384]{2,0,1:T(8,128)(2,1)}) %all-gather.7.cloned.1.call-update) | async-done | bytes 7077904 | tf_op jit(solution)/shard_map/all_gather | solution.py:130
  187.0 10.1 %copy.66 = bf16[3072,3,384]{0,2,1:T(8,128)(2,1)} copy(bf16[3072,3,384]{2,0,1:T(8,128)(2,1)} %all-gather.7.cloned.1.call-done) | data formatting | bytes 14155776 | tf_op jit(solution)/shard_map/all_gather | solution.py:130
  197.1 6.3 %fusion.29 = f32[512,3,4,96]{0,3,2,1:T(8,128)S(1)} fusion(bf16[3,4,96,3072]{3,2,1,0:T(8,128)(2,1)} %bitcast.139, bf16[1,512,3072]{2,1,0:T(8,128)(2,1)S(1)} %copy-done.1, f32[3072]{0:T(1024)S(1)} %convert_element_type.79, f32[512]{0:T(512)S(1)} %add_rsqrt_fusion), kind=kOutput, calls=%fused_computation.44 | convolution fusion | flops 3630170112 | bytes 12597248 | tf_op jit(solution)/shard_map/dot_general | solution.py:131
  203.6 0.3 subtract_convert_fusion
  203.9 1.1 maximum_maximum_fusion
  205.1 0.5 all-gather.11.cloned.1.call-update
  205.7 40.3 %all-gather.9.cloned.1.call-done = bf16[2,3072,384]{1,2,0:T(8,128)(2,1)} async-done(((bf16[2,768,384]{1,2,0:T(8,128)(2,1)}), bf16[2,3072,384]{1,2,0:T(8,128)(2,1)}) %all-gather.9.cloned.1.call-update) | async-done | bytes 4718608 | tf_op jit(solution)/shard_map/all_gather | solution.py:190
  246.0 53.0 %while.20 = (s32[]{:T(128)}, f32[4,512]{1,0:T(4,128)S(1)}, f32[4,512]{1,0:T(4,128)S(1)}, f32[512,4,96]{0,2,1:T(8,128)S(1)}, s32[]{:T(128)}, /*index=5*/bf16[2,30...) while((s32[]{:T(128)}, f32[4,512]{1,0:T(4,128)S(1)}, ...), condition=%wide.region_4.5_spmd.clone, body=%wide.region_1.4_spmd.clone.sunk | while | flops 625841408 | bytes 51262716 | solution.py:197
  246.0 0.6 add_compare_fusion.2
  246.6 0.7 compare_select_fusion.6
  247.3 1.3 constant_dynamic-slice_fusion.3
  248.7 4.0 fusion.88
  252.7 4.5 %fusion.90 = f32[4,512]{1,0:T(4,128)S(1)} fusion(f32[4,768,512]{2,1,0:T(8,128)} %get-tuple-element.349, f32[4,512]{1,0:T(4,128)S(1)} %get-tuple-element.379, pred[512,768]{0,1:T(8,128)(4,1)S(1)} %compare_select_fusion.6), kind=kLoop, calls=%fused_computation.7.clone.1 | loop fusion | flops 7862272 | bytes 6701056 | tf_op jit(solution)/shard_map/while/body/eval_jaxpr/reduce_sum | solution.py:175
  257.3 1.9 fusion.92
  259.2 0.6 add_compare_fusion.2
  259.8 0.7 compare_select_fusion.6
  260.6 1.3 constant_dynamic-slice_fusion.3
  261.9 4.0 fusion.88
  266.0 4.5 %fusion.90 = f32[4,512]{1,0:T(4,128)S(1)} fusion(f32[4,768,512]{2,1,0:T(8,128)} %get-tuple-element.349, f32[4,512]{1,0:T(4,128)S(1)} %get-tuple-element.379, pred[512,768]{0,1:T(8,128)(4,1)S(1)} %compare_select_fusion.6), kind=kLoop, calls=%fused_computation.7.clone.1 | loop fusion | flops 7862272 | bytes 6701056 | tf_op jit(solution)/shard_map/while/body/eval_jaxpr/reduce_sum | solution.py:175
  270.5 1.9 fusion.92
  272.5 0.6 add_compare_fusion.2
  273.1 0.7 compare_select_fusion.6
  273.8 1.3 constant_dynamic-slice_fusion.3
  275.2 4.0 fusion.88
  279.2 4.5 %fusion.90 = f32[4,512]{1,0:T(4,128)S(1)} fusion(f32[4,768,512]{2,1,0:T(8,128)} %get-tuple-element.349, f32[4,512]{1,0:T(4,128)S(1)} %get-tuple-element.379, pred[512,768]{0,1:T(8,128)(4,1)S(1)} %compare_select_fusion.6), kind=kLoop, calls=%fused_computation.7.clone.1 | loop fusion | flops 7862272 | bytes 6701056 | tf_op jit(solution)/shard_map/while/body/eval_jaxpr/reduce_sum | solution.py:175
  283.8 1.9 fusion.92
  285.7 0.6 add_compare_fusion.2
  286.3 0.7 compare_select_fusion.6
  287.1 1.3 constant_dynamic-slice_fusion.3
  288.4 4.0 fusion.88
  292.5 4.5 %fusion.90 = f32[4,512]{1,0:T(4,128)S(1)} fusion(f32[4,768,512]{2,1,0:T(8,128)} %get-tuple-element.349, f32[4,512]{1,0:T(4,128)S(1)} %get-tuple-element.379, pred[512,768]{0,1:T(8,128)(4,1)S(1)} %compare_select_fusion.6), kind=kLoop, calls=%fused_computation.7.clone.1 | loop fusion | flops 7862272 | bytes 6701056 | tf_op jit(solution)/shard_map/while/body/eval_jaxpr/reduce_sum | solution.py:175
  297.0 1.9 fusion.92
  299.0 29.6 %all-gather.11.cloned.1.call-done = bf16[3072,384]{1,0:T(8,128)(2,1)} async-done(((bf16[96,384]{1,0:T(8,128)(2,1)}), bf16[3072,384]{1,0:T(8,128)(2,1)}) %all-gather.11.cloned.1.call-update) | async-done | bytes 2359312 | tf_op jit(solution)/shard_map/all_gather | solution.py:205
  328.6 3.5 convolution_convert_fusion
  332.2 2.8 copy.92
  335.1 1.2 fusion.63
  336.3 0.2 copy.69
  336.5 0.2 copy.68
  337.0 0.2 convert_reduce_fusion
  337.3 40.3 %all_gather.28 = bf16[256,768]{1,0:T(8,128)(2,1)S(1)} all-gather(bf16[8,768]{1,0:T(8,128)(2,1)S(1)} %bitcast.154), channel_id=1, replica_groups=mesh['grp'=8,'req'=4,'tp'=8] {'grp','req'}, dimensions={0}, use_global_device_ids=true | all-gather | bytes 405504 | tf_op jit(solution)/shard_map/all_gather | solution.py:242
  377.5 0.6 gather_fusion
  378.5 0.3 fusion.66
  378.8 0.2 fusion.38
  379.2 0.3 convolution_bitcast_fusion
  379.6 9.2 %all-gather.1 = f32[64,2,4,98]{3,0,2,1:T(8,128)S(1)} all-gather(f32[16,2,4,98]{3,0,2,1:T(8,128)S(1)} %pad_maximum_fusion.2), channel_id=3, replica_groups=mesh['grp'=8,'req'=4,'tp'=8] {'req'}, dimensions={0}, use_global_device_ids=true | all-gather | bytes 250880 | tf_op jit(solution)/shard_map/all_gather | solution.py:256
  388.9 0.2 fusion.64
  389.0 0.3 copy.95
  389.3 0.3 copy.96
  389.9 0.2 fusion.36
  390.5 20.9 %all_gather.31 = f32[128,2,4,98]{3,2,1,0:T(4,128)S(1)} all-gather(f32[16,2,4,98]{3,2,1,0:T(4,128)S(1)} %copy.77), channel_id=1, replica_groups=mesh['grp'=8,'req'=4,'tp'=8] {'grp'}, dimensions={0}, use_global_device_ids=true | all-gather | bytes 451584 | tf_op jit(solution)/shard_map/all_gather | solution.py:265
  411.4 0.6 gather_fusion.1
  413.1 0.2 select_convert_fusion
  413.2 0.7 broadcast_in_dim_reshape.9
  413.9 1.9 copy.93
  (104 shorter events, 4.0 us)
Async XLA Ops:
  7.2 80.0 %all-gather.13.cloned.1.call-start = ((), (), s32[]{:S(2)}) async-start(), calls=%async_computation.4 | async-start | bytes 3538944 | tf_op jit(solution)/shard_map/all_gather | solution.py:124
  7.9 179.1 %all-gather.7.cloned.1.call-start = ((), (), s32[]{:S(2)}) async-start(), calls=%async_computation.1 | async-start | bytes 7299072 | tf_op jit(solution)/shard_map/all_gather | solution.py:130
  8.6 237.3 %all-gather.9.cloned.1.call-start = ((), (), s32[]{:S(2)}) async-start(), calls=%async_computation.2 | async-start | bytes 5898240 | tf_op jit(solution)/shard_map/all_gather | solution.py:190
  89.8 107.3 %copy-start.1 = (bf16[1,512,3072]{2,1,0:T(8,128)(2,1)S(1)}, bf16[1,512,3072]{2,1,0:T(8,128)(2,1)}, u32[]{:S(2)}) copy-start(bf16[1,512,3072]{2,1,0:T(8,128)(2,1)} %all-gather.13.cloned.1.call-done) | copy-start | bytes 9437188
  197.1 6.5 %copy-start.2 = (f32[512,48]{0,1:T(8,128)S(1)}, f32[512,48]{0,1:T(8,128)}, u32[]{:S(2)}) copy-start(f32[512,48]{0,1:T(8,128)} %get-tuple-element.283) | copy-start | bytes 294916
  197.1 6.5 %copy-start.3 = (f32[512,48]{0,1:T(8,128)S(1)}, f32[512,48]{0,1:T(8,128)}, u32[]{:S(2)}) copy-start(f32[512,48]{0,1:T(8,128)} %get-tuple-element.284) | copy-start | bytes 294916
  205.0 123.6 %all-gather.11.cloned.1.call-start = ((), (), s32[]{:S(2)}) async-start(), calls=%async_computation.3 | async-start | bytes 2433024 | tf_op jit(solution)/shard_map/all_gather | solution.py:205
  205.6 208.3 %reduce-scatter.4.cloned.1.call-start = ((), (), s32[]{:S(2)}) async-start(), calls=%async_computation.5 | async-start | bytes 3538944
  252.7 4.6 %copy-start = (f32[4,768,512]{2,1,0:T(8,128)S(1)}, f32[4,768,512]{2,1,0:T(8,128)}, u32[]{:S(2)}) copy-start(f32[4,768,512]{2,1,0:T(8,128)} %get-tuple-element.349) | copy-start | bytes 18874372 | tf_op jit(solution)/shard_map/while
  265.9 4.6 %copy-start = (f32[4,768,512]{2,1,0:T(8,128)S(1)}, f32[4,768,512]{2,1,0:T(8,128)}, u32[]{:S(2)}) copy-start(f32[4,768,512]{2,1,0:T(8,128)} %get-tuple-element.349) | copy-start | bytes 18874372 | tf_op jit(solution)/shard_map/while
  279.2 4.6 %copy-start = (f32[4,768,512]{2,1,0:T(8,128)S(1)}, f32[4,768,512]{2,1,0:T(8,128)}, u32[]{:S(2)}) copy-start(f32[4,768,512]{2,1,0:T(8,128)} %get-tuple-element.349) | copy-start | bytes 18874372 | tf_op jit(solution)/shard_map/while
  292.4 4.6 %copy-start = (f32[4,768,512]{2,1,0:T(8,128)S(1)}, f32[4,768,512]{2,1,0:T(8,128)}, u32[]{:S(2)}) copy-start(f32[4,768,512]{2,1,0:T(8,128)} %get-tuple-element.349) | copy-start | bytes 18874372 | tf_op jit(solution)/shard_map/while
  332.1 2.9 copy-start.4
  332.1 4.6 %copy-start.6 = (s32[8,16]{1,0:T(8,128)S(1)}, s32[8,16]{1,0:T(8,128)}, u32[]{:S(2)}) copy-start(s32[8,16]{1,0:T(8,128)} %param.20) | copy-start | bytes 1540
  332.1 4.7 %copy-start.8 = (s32[8]{0:T(128)S(1)}, s32[8]{0:T(128)}, u32[]{:S(2)}) copy-start(s32[8]{0:T(128)} %param.19) | copy-start | bytes 100
  332.2 46.1 %copy-start.7 = (s32[8,16]{1,0:T(8,128)S(1)}, s32[8,16]{1,0:T(8,128)}, u32[]{:S(2)}) copy-start(s32[8,16]{1,0:T(8,128)} %param.21) | copy-start | bytes 1540
  335.0 55.2 %copy-start.5 = (bf16[1,8,2,2,384]{4,3,2,1,0:T(2,128)(2,1)S(1)}, bf16[1,8,2,2,384]{4,3,2,1,0:T(2,128)(2,1)}, u32[]{:S(2)}) copy-start(bf16[1,8,2,2,384]{4,3,2,1,0:T(2,128)(2,1)} %param.23) | copy-start | bytes 73732
Sparse Core Ops, SparseCore 0:
  9.8 77.3 all-gather.12
  90.0 96.9 all-gather.6
  205.1 40.7 all-gather.8
  248.6 79.9 all-gather.10
  335.1 75.4 reduce-scatter.3
